TPU v7x, 256 devices: a whole 4x4x8 slice. The times are simulated.
256 devices in a mesh: section: 2 (over core), tok: 32 (over z, y), rep: 4 (over x).
Axes of the slice: x: 4, y: 4, z: 8, core: 2. Of those that a mesh axis runs over, the one named last changes fastest.
Arguments:
- inputs: bfloat16 [2, 4096, 1024], P(None, 'tok')
- segment_ids: int32 [2, 4096], replicated, may hold values from 0 to 7, as said below
- picks: int32 [2, 4096, 2], P(None, 'tok'), may hold values from 0 to 15, all different within a row; in each aligned block of 128 rows (0 to 127, 128 to 255, ..., all dimensions but the last counted through in order) at most 20 rows name the same one
- page_table: int32 [2, 32], replicated, may hold values from 0 to 31, each once within a row
- norm_gains: float32 [2, 2, 1024], P('section'), may hold values from 0.1 to 1.9
- attn_qkv: bfloat16 [2, 1024, 3, 1024], P('section', None, None, 'rep')
- attn_out: bfloat16 [2, 1024, 1024], P('section', 'rep'), may hold values from -0.1875 to 0.1875
- router: bfloat16 [2, 1024, 16], P('section')
- expert_in: bfloat16 [2, 32, 1024, 2, 1408], P('section', 'tok', None, None, 'rep'), may hold values from -0.1875 to 0.1875
- expert_out: bfloat16 [2, 32, 1408, 1024], P('section', 'tok', 'rep')
Outputs:
- layer_out: bfloat16 [2, 2, 4096, 1024], P('section', None, 'tok')
- kv_pages: bfloat16 [2, 2, 32, 128, 2, 1024], P('section', None, 'tok', None, None, 'rep')
Inputs may be any that keep to these rules, and one draw needn't show every extreme that they name: `picks`: within the tokens of one index of tok in one micro-batch, at most 20 tokens pick one expert, and some expert is picked by exactly 20. `segment_ids`: ids never fall along a micro-batch; every prompt has at least one token, a prompt spans at most 2048 tokens and one spans exactly 2048. `page_table`: each row is a permutation.
All inputs are finite; a program needn't handle non-finite values.
Results may differ from a plain program's by a relative error of at most 0.034.
Values may be sent and summed in bfloat16 or wider, within the bound.
No kernel may reach another device: no remote copies, remote signals or barrier semaphores. Data moves between devices by JAX's collectives and lax.ppermute only.
A program may use at most 128 MiB of HBM per device.

v0:
```python
import jax
import jax.numpy as jnp
from jax import lax
from jax.sharding import PartitionSpec as P

HEAD_DIM = 64
TOP = 2
PAGE = 128
CAP = 20
NEG_FILL = -1e30


def shifted(value, axis, steps):
    count = lax.axis_size(axis)
    first, last = (max(0, -steps), min(count, count - steps))
    return lax.ppermute(value, axis, [(source, source + steps) for source in range(first, last)])


def rms_scale(values, gains):
    return values * lax.rsqrt(jnp.mean(values * values, axis=-1, keepdims=True) + 1e-06) * gains


def attend(carry, queries, keys_vals, seg_query, pos_query, seg_key, pos_key):
    run_max, run_sum, run_acc = carry
    heads_here = run_acc.shape[0]
    head_size = run_acc.shape[2]
    rows_key = keys_vals.shape[0]
    key_part = keys_vals[:, 0].reshape(rows_key, heads_here, head_size)
    val_part = keys_vals[:, 1].reshape(rows_key, heads_here, head_size).astype(jnp.float32)
    scores = jnp.einsum(
        "thd,nhd->htn", queries, key_part, preferred_element_type=jnp.float32
    ) * head_size ** (-0.5)
    visible = (seg_query[:, None] == seg_key[None, :]) & (pos_query[:, None] >= pos_key[None, :])
    masked = jnp.where(visible[None], scores, NEG_FILL)
    new_max = jnp.maximum(run_max, jnp.max(masked, axis=-1))
    weights = jnp.where(visible[None], jnp.exp(masked - new_max[..., None]), 0.0)
    decay = jnp.exp(run_max - new_max)
    run_sum = run_sum * decay + jnp.sum(weights, axis=-1)
    run_acc = run_acc * decay[..., None] + jnp.einsum(
        "htn,nhd->htd", weights, val_part, precision=lax.Precision.HIGHEST
    )
    return (new_max, run_sum, run_acc)


def place_pages(pages, keys_vals, table_row, tok_index):
    rows_here = keys_vals.shape[0]
    blocks_dev = pages.shape[0]
    page_rows = pages.shape[1]
    block_ids = jnp.arange(table_row.shape[0], dtype=jnp.int32)
    wanted = tok_index * blocks_dev + 0
    source = jnp.sum(jnp.where(table_row == wanted, block_ids, 0))
    offset = source * page_rows
    inside = (offset >= 0) & (offset + page_rows <= rows_here)
    block = lax.dynamic_slice_in_dim(
        keys_vals, jnp.clip(offset, 0, rows_here - page_rows), page_rows, 0
    )
    updated = [jnp.where(inside, block, pages[0])]
    return jnp.stack(updated)


def per_device(
    inputs,
    segment_ids,
    picks,
    page_table,
    norm_gains,
    attn_qkv,
    attn_out,
    router,
    expert_in,
    expert_out,
):
    section_index = lax.axis_index("section")
    tok_index = lax.axis_index("tok")
    tok_count = lax.axis_size("tok")
    micro_count = inputs.shape[0]
    tok_rows = inputs.shape[1]
    width = inputs.shape[2]
    col_width = attn_qkv.shape[3]
    head_count = col_width // HEAD_DIM
    experts_all = router.shape[2]
    local_pieces = expert_in.shape[1]
    split_count = local_pieces * tok_count // experts_all
    blocks_dev = tok_rows // PAGE
    row_ids = jnp.arange(tok_rows, dtype=jnp.int32)
    pos_query = tok_index * tok_rows + row_ids
    gains = norm_gains[0]
    w_qkv = attn_qkv[0].reshape(width, 3 * col_width)
    w_out = attn_out[0]
    w_router = router[0]
    w_in = expert_in[0]
    w_down = expert_out[0]
    outputs = [jnp.zeros((tok_rows, width), jnp.bfloat16) for slot_micro in range(micro_count)]
    page_out = [
        jnp.zeros((blocks_dev, PAGE, 2, col_width), jnp.bfloat16)
        for slot_micro in range(micro_count)
    ]
    received = jnp.zeros((tok_rows, width), jnp.bfloat16)
    for round_index in range(micro_count + 1):
        own_micro = round_index - section_index
        micro_index = jnp.clip(own_micro, 0, micro_count - 1)
        fresh = inputs[min(round_index, micro_count - 1)]
        layer_in = jnp.where(section_index == 0, fresh, received)
        seg_all = lax.dynamic_index_in_dim(segment_ids, micro_index, 0, keepdims=False)
        seg_query = lax.dynamic_slice_in_dim(seg_all, tok_index * tok_rows, tok_rows)
        table_row = lax.dynamic_index_in_dim(page_table, micro_index, 0, keepdims=False)
        pick_rows = lax.dynamic_index_in_dim(picks, micro_index, 0, keepdims=False)
        resid = layer_in.astype(jnp.float32)
        normed = rms_scale(resid, gains[0]).astype(jnp.bfloat16)
        projected = jnp.dot(normed, w_qkv, preferred_element_type=jnp.float32).astype(jnp.bfloat16)
        projected = projected.reshape(tok_rows, 3, col_width)
        queries = projected[:, 0].reshape(tok_rows, head_count, HEAD_DIM)
        keys_vals = projected[:, 1:]
        soft_init = (
            jnp.full((head_count, tok_rows), NEG_FILL, jnp.float32),
            jnp.zeros((head_count, tok_rows), jnp.float32),
            jnp.zeros((head_count, tok_rows, HEAD_DIM), jnp.float32),
        )
        empty_pages = jnp.zeros((blocks_dev, PAGE, 2, col_width), jnp.bfloat16)
        piece = lax.all_gather(keys_vals, "tok", axis=0, tiled=True)
        rows_key = piece.shape[0]
        step_rows = 1024
        while rows_key % step_rows != 0:
            step_rows = step_rows // 2
        turns = rows_key // step_rows

        def key_block(index, soft_now):
            start = index * step_rows
            block = lax.dynamic_slice_in_dim(piece, start, step_rows, 0)
            seg_key = lax.dynamic_slice_in_dim(seg_all, start, step_rows)
            pos_key = start + jnp.arange(step_rows, dtype=jnp.int32)
            return attend(soft_now, queries, block, seg_query, pos_query, seg_key, pos_key)

        soft_next = lax.fori_loop(0, turns, key_block, soft_init)
        pages = place_pages(empty_pages, piece, table_row, tok_index)
        run_max, run_sum, run_acc = soft_next
        context = (
            (run_acc / run_sum[..., None])
            .transpose(1, 0, 2)
            .reshape(tok_rows, col_width)
            .astype(jnp.bfloat16)
        )
        attn_part = jnp.dot(context, w_out, preferred_element_type=jnp.float32)
        mid = resid + lax.psum(attn_part, "rep")
        normed_mid = rms_scale(mid, gains[1]).astype(jnp.bfloat16)
        logits = jnp.dot(normed_mid, w_router, preferred_element_type=jnp.float32)
        expert_ids = jnp.arange(experts_all, dtype=jnp.int32)
        chosen = (pick_rows[:, :, None] == expert_ids[None, None, :]).astype(jnp.int32)
        picked_logit = jnp.sum(chosen.astype(jnp.float32) * logits[:, None, :], axis=-1)
        top_logit = jnp.max(picked_logit, axis=-1, keepdims=True)
        raised = jnp.exp(picked_logit - top_logit)
        gate_vals = raised / jnp.sum(raised, axis=-1, keepdims=True)
        ordered = chosen.transpose(1, 0, 2).reshape(TOP * tok_rows, experts_all)
        slot_of = jnp.sum((jnp.cumsum(ordered, axis=0) - 1) * ordered, axis=-1)
        flat_slot = pick_rows.T.reshape(TOP * tok_rows) * CAP + slot_of
        slot_ids = jnp.arange(experts_all * CAP, dtype=jnp.int32)
        hits = (flat_slot[:, None] == slot_ids[None, :]).astype(jnp.int32)
        hits = jnp.sum(hits.reshape(TOP, tok_rows, experts_all * CAP), axis=0).astype(jnp.bfloat16)
        dispatch = lax.dot_general(
            hits, normed_mid, (((0,), (0,)), ((), ())), preferred_element_type=jnp.float32
        ).astype(jnp.bfloat16)
        copies = jnp.broadcast_to(
            dispatch.reshape(experts_all, 1, CAP, width), (experts_all, split_count, CAP, width)
        )
        copies = copies.reshape(tok_count, local_pieces, CAP, width)
        act = jnp.einsum(
            "secd,edgf->secgf",
            lax.all_to_all(copies, "tok", split_axis=0, concat_axis=0, tiled=True),
            w_in,
            preferred_element_type=jnp.float32,
        )
        hidden = (jax.nn.gelu(act[..., 0, :]) * act[..., 1, :]).astype(jnp.bfloat16)
        returned = lax.all_to_all(
            jnp.einsum("secf,efd->secd", hidden, w_down, preferred_element_type=jnp.float32).astype(
                jnp.bfloat16
            ),
            "tok",
            split_axis=0,
            concat_axis=0,
            tiled=True,
        )
        summed = jnp.sum(
            returned.reshape(experts_all, split_count, CAP, width).astype(jnp.float32), axis=1
        )
        summed = summed.reshape(experts_all * CAP, width)
        gathered = jnp.take(summed, flat_slot, axis=0).reshape(TOP, tok_rows, width)
        expert_local = jnp.sum(gate_vals.T[:, :, None] * gathered, axis=0)
        expert_total = lax.psum(expert_local, "rep")
        layer_result = (mid + expert_total).astype(jnp.bfloat16)
        for slot_micro in range(micro_count):
            if slot_micro == round_index or slot_micro == round_index - 1:
                taken = own_micro == slot_micro
                outputs[slot_micro] = jnp.where(taken, layer_result, outputs[slot_micro])
                page_out[slot_micro] = jnp.where(taken, pages, page_out[slot_micro])
        if round_index < micro_count:
            received = shifted(layer_result, "section", 1)
    return (jnp.stack(outputs)[None], jnp.stack(page_out)[None])


def solution(mesh):
    return jax.shard_map(
        per_device,
        mesh=mesh,
        in_specs=(
            P(None, "tok", None),
            P(),
            P(None, "tok", None),
            P(),
            P("section", None, None),
            P("section", None, None, "rep"),
            P("section", "rep", None),
            P("section", None, None),
            P("section", "tok", None, None, "rep"),
            P("section", "tok", "rep", None),
        ),
        out_specs=(P("section", None, "tok", None), P("section", None, "tok", None, None, "rep")),
        check_vma=False,
    )
```

profile of v0, /device:TPU:8, one launch (start us, length us, event | category | flops | bytes accessed | tf_op | source)
XLA Modules:
  0.0 1003.8 jit_solution(15672951469307340651)
XLA Ops:
  20.4 79.9 %all-gather.4.cloned.1.call-done = bf16[4096,2,256]{0,2,1:T(8,128)(2,1)} async-done(((bf16[128,2,256]{0,2,1:T(8,128)(2,1)}), bf16[4096,2,256]{0,2,1:T(8,128)(2,1)}) %all-gather.4.cloned.1.call-update) | async-done | bytes 4194320 | tf_op jit(solution)/shard_map/all_gather | solution.py:120
  100.3 34.9 %while.54 = (s32[]{:T(128)}, f32[4,128]{1,0:T(4,128)S(1)}, f32[4,128]{1,0:T(4,128)S(1)}, f32[4,128,64]{1,2,0:T(8,128)}, s32[128]{0:T(128)}, /*index=5*/s32[4096]...) while((s32[]{:T(128)}, f32[4,128]{1,0:T(4,128)S(1)}, ...), condition=%wide.region_4.5_spmd.clone, body=%wide.region_1.4_spmd.clone.sunk | while | flops 476548736 | bytes 14800775 | solution.py:134
  140.8 46.1 %all-reduce.7.cloned.1.call-done = f32[128,1024]{1,0:T(8,128)} async-done(((f32[128,1024]{1,0:T(8,128)}), f32[128,1024]{1,0:T(8,128)}) %all-reduce.7.cloned.1.call-update) | async-done | bytes 524304 | tf_op jit(solution)/shard_map/psum | solution.py:144
  190.6 47.1 %all_to_all.30 = bf16[32,1,20,1024]{3,2,1,0:T(8,128)(2,1)S(1)} all-to-all(bf16[32,1,20,1024]{3,2,1,0:T(8,128)(2,1)S(1)} %bitcast.386), channel_id=1, replica_groups=mesh['section'=2,'tok'=32,'rep'=4] {'tok'}, dimensions={0} | all-to-all | bytes 2621440 | tf_op jit(solution)/shard_map/all_to_all | solution.py:168
  242.3 5.7 all-to-all-start.1
  251.2 33.0 %all-to-all-done.1 = bf16[32,1,20,1024]{3,2,1,0:T(8,128)(2,1)S(1)} async-done(((bf16[32,1,20,1024]{3,2,1,0:T(8,128)(2,1)}), bf16[32,1,20,1024]{3,2,1,0:T(8,128)(2,1)S(1)}, u32[]{:S(2)}, u32[]{:S(2)}) %all-to-all-start.1) | async-done | bytes 1310752 | tf_op jit(solution)/shard_map/all_to_all | solution.py:173
  287.2 2.2 gather_fusion
  291.7 45.9 %all-reduce.9.cloned.1.call-done = f32[128,1024]{1,0:T(8,128)} async-done(((f32[128,1024]{1,0:T(8,128)}), f32[128,1024]{1,0:T(8,128)}) %all-reduce.9.cloned.1.call-update) | async-done | bytes 524304 | tf_op jit(solution)/shard_map/psum | solution.py:188
  348.5 79.2 %all-gather.6.cloned.1.call-done = bf16[4096,2,256]{0,2,1:T(8,128)(2,1)} async-done(((bf16[128,2,256]{0,2,1:T(8,128)(2,1)}), bf16[4096,2,256]{0,2,1:T(8,128)(2,1)}) %all-gather.6.cloned.1.call-update) | async-done | bytes 4194320 | tf_op jit(solution)/shard_map/all_gather | solution.py:120
  427.7 35.0 %while.55 = (s32[]{:T(128)}, f32[4,128]{1,0:T(4,128)S(1)}, f32[4,128]{1,0:T(4,128)S(1)}, f32[4,128,64]{1,2,0:T(8,128)}, s32[128]{0:T(128)}, /*index=5*/s32[4096]...) while((s32[]{:T(128)}, f32[4,128]{1,0:T(4,128)S(1)}, ...), condition=%wide.region_21.23_spmd.clone, body=%wide.region_18.22_spmd.clone.sunk | while | flops 476548736 | bytes 14800775 | solution.py:134
  468.8 45.5 %all-reduce.11.cloned.1.call-done = f32[128,1024]{1,0:T(8,128)} async-done(((f32[128,1024]{1,0:T(8,128)}), f32[128,1024]{1,0:T(8,128)}) %all-reduce.11.cloned.1.call-update) | async-done | bytes 524304 | tf_op jit(solution)/shard_map/psum | solution.py:144
  517.3 47.1 %all_to_all.31 = bf16[32,1,20,1024]{3,2,1,0:T(8,128)(2,1)S(1)} all-to-all(bf16[32,1,20,1024]{3,2,1,0:T(8,128)(2,1)S(1)} %bitcast.387), channel_id=1, replica_groups=mesh['section'=2,'tok'=32,'rep'=4] {'tok'}, dimensions={0} | all-to-all | bytes 2621440 | tf_op jit(solution)/shard_map/all_to_all | solution.py:168
  569.0 5.7 all-to-all-start.3
  577.6 33.2 %all-to-all-done.3 = bf16[32,1,20,1024]{3,2,1,0:T(8,128)(2,1)S(1)} async-done(((bf16[32,1,20,1024]{3,2,1,0:T(8,128)(2,1)}), bf16[32,1,20,1024]{3,2,1,0:T(8,128)(2,1)S(1)}, u32[]{:S(2)}, u32[]{:S(2)}) %all-to-all-start.3) | async-done | bytes 1310752 | tf_op jit(solution)/shard_map/all_to_all | solution.py:173
  613.8 2.2 gather_fusion.1
  618.5 46.1 %all-reduce.13.cloned.1.call-done = f32[128,1024]{1,0:T(8,128)} async-done(((f32[128,1024]{1,0:T(8,128)}), f32[128,1024]{1,0:T(8,128)}) %all-reduce.13.cloned.1.call-update) | async-done | bytes 524304 | tf_op jit(solution)/shard_map/psum | solution.py:188
  672.4 82.9 %all-gather.8.cloned.1.call-done = bf16[4096,2,256]{0,2,1:T(8,128)(2,1)} async-done(((bf16[128,2,256]{0,2,1:T(8,128)(2,1)}), bf16[4096,2,256]{0,2,1:T(8,128)(2,1)}) %all-gather.8.cloned.1.call-update) | async-done | bytes 4194320 | tf_op jit(solution)/shard_map/all_gather | solution.py:120
  755.3 34.7 %while.56 = (s32[]{:T(128)}, f32[4,128]{1,0:T(4,128)S(1)}, f32[4,128]{1,0:T(4,128)S(1)}, f32[4,128,64]{1,2,0:T(8,128)}, s32[128]{0:T(128)}, /*index=5*/s32[4096]...) while((s32[]{:T(128)}, f32[4,128]{1,0:T(4,128)S(1)}, ...), condition=%wide.region_38.40_spmd.clone, body=%wide.region_35.39_spmd.clone.sunk | while | flops 476548736 | bytes 14800775 | solution.py:134
  793.9 47.8 %all-reduce.15.cloned.1.call-done = f32[128,1024]{1,0:T(8,128)} async-done(((f32[128,1024]{1,0:T(8,128)}), f32[128,1024]{1,0:T(8,128)}) %all-reduce.15.cloned.1.call-update) | async-done | bytes 524304 | tf_op jit(solution)/shard_map/psum | solution.py:144
  846.6 47.1 %all_to_all.32 = bf16[32,1,20,1024]{3,2,1,0:T(8,128)(2,1)S(1)} all-to-all(bf16[32,1,20,1024]{3,2,1,0:T(8,128)(2,1)S(1)} %bitcast.388), channel_id=1, replica_groups=mesh['section'=2,'tok'=32,'rep'=4] {'tok'}, dimensions={0} | all-to-all | bytes 2621440 | tf_op jit(solution)/shard_map/all_to_all | solution.py:168
  898.3 5.9 all-to-all-start.5
  904.6 35.8 %all-to-all-done.5 = bf16[32,1,20,1024]{3,2,1,0:T(8,128)(2,1)} async-done(((bf16[32,1,20,1024]{3,2,1,0:T(8,128)(2,1)}), bf16[32,1,20,1024]{3,2,1,0:T(8,128)(2,1)}, u32[]{:S(2)}, u32[]{:S(2)}) %all-to-all-start.5) | async-done | bytes 1310752 | tf_op jit(solution)/shard_map/all_to_all | solution.py:173
  940.3 3.1 convert_reduce_fusion
  954.1 41.2 %all-reduce.17.cloned.1.call-done = f32[128,1024]{1,0:T(8,128)} async-done(((f32[128,1024]{1,0:T(8,128)}), f32[128,1024]{1,0:T(8,128)}) %all-reduce.17.cloned.1.call-update) | async-done | bytes 524304 | tf_op jit(solution)/shard_map/psum | solution.py:188
  (497 shorter events, 204.1 us)
Async XLA Ops:
  7.2 230.5 %copy-start = (bf16[1,1,1024,2,352]{2,4,3,1,0:T(8,128)(2,1)S(1)}, bf16[1,1,1024,2,352]{2,4,3,1,0:T(8,128)(2,1)}, u32[]{:S(2)}) copy-start(bf16[1,1,1024,2,352]{2,4,3,1,0:T(8,128)(2,1)} %param.26) | copy-start | bytes 4325380
  7.2 93.1 %all-gather.4.cloned.1.call-start = ((), (), s32[]{:S(2)}) async-start(), calls=%async_computation.6 | async-start | bytes 4325376 | tf_op jit(solution)/shard_map/all_gather | solution.py:120
  11.0 89.3 %copy-start.7 = (bf16[1,1024,3,256]{1,3,2,0:T(8,128)(2,1)}, bf16[1,1024,3,256]{1,3,2,0:T(8,128)(2,1)S(1)}, u32[]{:S(2)}) copy-start(bf16[1,1024,3,256]{1,3,2,0:T(8,128)(2,1)S(1)} %copy.83) | copy-start | bytes 4718596
  14.2 172.7 %all-reduce.7.cloned.1.call-start = ((), (), s32[]{:S(2)}) async-start(), calls=%async_computation.7 | async-start | bytes 1048576 | tf_op jit(solution)/shard_map/psum | solution.py:144
  16.2 84.1 %copy-start.45 = (s32[2,128]{1,0:T(2,128)}, s32[2,128]{1,0:T(2,128)S(1)}, u32[]{:S(2)}) copy-start(s32[2,128]{1,0:T(2,128)S(1)} %get-tuple-element.708) | copy-start | bytes 3076
  135.2 51.6 %copy-start.18 = (bf16[2,128,1024]{2,1,0:T(8,128)(2,1)S(1)}, bf16[2,128,1024]{2,1,0:T(8,128)(2,1)}, u32[]{:S(2)}) copy-start(bf16[2,128,1024]{2,1,0:T(8,128)(2,1)} %param.18) | copy-start | bytes 1572868
  242.3 41.9 %all-to-all-start.1 = ((bf16[32,1,20,1024]{3,2,1,0:T(8,128)(2,1)}), bf16[32,1,20,1024]{3,2,1,0:T(8,128)(2,1)S(1)}, u32[]{:S(2)}, u32[]{:S(2)}) async-start(bf16[32,1,20,1024]{3,2,1,0:T(8,128)(2,1)} %copy.87), calls=%async_computation.1 | async-start | bytes 3145728 | tf_op jit(solution)/shard_map/all_to_all | solution.py:173
  248.0 89.7 %all-reduce.9.cloned.1.call-start = ((), (), s32[]{:S(2)}) async-start(), calls=%async_computation.8 | async-start | bytes 1048576 | tf_op jit(solution)/shard_map/psum | solution.py:188
  290.7 51.6 %copy-start.8 = (bf16[1,1024,3,256]{1,3,2,0:T(8,128)(2,1)S(1)}, bf16[1,1024,3,256]{1,3,2,0:T(8,128)(2,1)}, u32[]{:S(2)}) copy-start(bf16[1,1024,3,256]{1,3,2,0:T(8,128)(2,1)} %copy-done.7) | copy-start | bytes 4718596
  291.7 136.0 %all-gather.6.cloned.1.call-start = ((), (), s32[]{:S(2)}) async-start(), calls=%async_computation.9 | async-start | bytes 4325376 | tf_op jit(solution)/shard_map/all_gather | solution.py:120
  339.0 2.4 collective-permute-start
  343.9 170.4 %all-reduce.11.cloned.1.call-start = ((), (), s32[]{:S(2)}) async-start(), calls=%async_computation.10 | async-start | bytes 1048576 | tf_op jit(solution)/shard_map/psum | solution.py:144
  345.2 82.5 %copy-start.31 = (s32[16,2,128]{2,0,1:T(8,128)}, s32[16,2,128]{2,0,1:T(8,128)S(1)}, u32[]{:S(2)}) copy-start(s32[16,2,128]{2,0,1:T(8,128)S(1)} %reduce-window.24) | copy-start | bytes 49156
  462.7 51.6 %copy-start.16 = (bf16[128,1024]{1,0:T(8,128)(2,1)S(1)}, bf16[128,1024]{1,0:T(8,128)(2,1)}, u32[]{:S(2)}) copy-start(bf16[128,1024]{1,0:T(8,128)(2,1)} %copy-done.15) | copy-start | bytes 786436
  569.0 41.9 %all-to-all-start.3 = ((bf16[32,1,20,1024]{3,2,1,0:T(8,128)(2,1)}), bf16[32,1,20,1024]{3,2,1,0:T(8,128)(2,1)S(1)}, u32[]{:S(2)}, u32[]{:S(2)}) async-start(bf16[32,1,20,1024]{3,2,1,0:T(8,128)(2,1)} %copy.93), calls=%async_computation.3 | async-start | bytes 3145728 | tf_op jit(solution)/shard_map/all_to_all | solution.py:173
  574.7 89.8 %all-reduce.13.cloned.1.call-start = ((), (), s32[]{:S(2)}) async-start(), calls=%async_computation.11 | async-start | bytes 1048576 | tf_op jit(solution)/shard_map/psum | solution.py:188
  618.4 51.6 %copy-start.9 = (bf16[1,1024,3,256]{1,3,2,0:T(8,128)(2,1)S(1)}, bf16[1,1024,3,256]{1,3,2,0:T(8,128)(2,1)}, u32[]{:S(2)}) copy-start(bf16[1,1024,3,256]{1,3,2,0:T(8,128)(2,1)} %copy-done.7) | copy-start | bytes 4718596
  618.4 51.6 %copy-start.40 = (f32[1,1,1024]{2,1,0:T(1,128)S(1)}, f32[1,1,1024]{2,1,0:T(1,128)}, u32[]{:S(2)}) copy-start(f32[1,1,1024]{2,1,0:T(1,128)} %copy-done.38) | copy-start | bytes 12292
  618.4 136.9 %all-gather.8.cloned.1.call-start = ((), (), s32[]{:S(2)}) async-start(), calls=%async_computation.12 | async-start | bytes 4325376 | tf_op jit(solution)/shard_map/all_gather | solution.py:120
  666.6 2.4 collective-permute-start.1
  671.5 170.2 %all-reduce.15.cloned.1.call-start = ((), (), s32[]{:S(2)}) async-start(), calls=%async_computation.13 | async-start | bytes 1048576 | tf_op jit(solution)/shard_map/psum | solution.py:144
  790.0 51.6 %copy-start.14 = (bf16[128,1024]{1,0:T(8,128)(2,1)S(1)}, bf16[128,1024]{1,0:T(8,128)(2,1)}, u32[]{:S(2)}) copy-start(bf16[128,1024]{1,0:T(8,128)(2,1)} %copy-done.13) | copy-start | bytes 786436
  898.3 42.0 %all-to-all-start.5 = ((bf16[32,1,20,1024]{3,2,1,0:T(8,128)(2,1)}), bf16[32,1,20,1024]{3,2,1,0:T(8,128)(2,1)}, u32[]{:S(2)}, u32[]{:S(2)}) async-start(bf16[32,1,20,1024]{3,2,1,0:T(8,128)(2,1)} %copy.99), calls=%async_computation.5 | async-start | bytes 3145728 | tf_op jit(solution)/shard_map/all_to_all | solution.py:173
  904.2 91.1 %all-reduce.17.cloned.1.call-start = ((), (), s32[]{:S(2)}) async-start(), calls=%async_computation.14 | async-start | bytes 1048576 | tf_op jit(solution)/shard_map/psum | solution.py:188
  (97 other events, 422.6 us)
Sparse Core Ops, SparseCore 0:
  14.3 85.9 all-gather.3
  138.5 48.3 all-reduce.6
  291.8 45.8 all-reduce.8
  344.0 83.6 all-gather.5
  465.9 48.3 all-reduce.10
  618.5 45.9 all-reduce.12
  671.6 83.6 all-gather.7
  793.3 48.3 all-reduce.14
  949.4 45.8 all-reduce.16
where the time goes:
time: 1010 us; the launch traced here: 1000 us
  waiting for transfers between devices  619 us (61%)
  blocking collectives  141 us (14%)
  other arithmetic  82.9 us (8%)
  local copies, waits for them, and re-layouts  77.7 us (8%)
  matrix products  45.3 us (4%)
  starting transfers between devices  20.6 us (2%)
  between operations  16.4 us (2%)
    all_gather x3, waiting for transfers between devices, per_device(): piece = lax.all_gather(keys_vals, 'tok', axis=0, tiled=True)  242 us
    all_to_all x3, blocking collectives, per_device(): lax.all_to_all(copies, 'tok', split_axis=0, concat_axis=0, tiled=True)  141 us
    psum x3, waiting for transfers between devices, per_device(): mid = resid + lax.psum(attn_part, 'rep')  139 us
    psum x3, waiting for transfers between devices, per_device(): expert_total = lax.psum(expert_local, 'rep')  133 us
    all_to_all x3, waiting for transfers between devices, per_device(): lax.all_to_all(jnp.einsum('secf,efd->secd', hidden, w_down, preferred_ele...  102 us
    slice x12, local copies, waits for them, and re-layouts, attend(): keys_vals[:, 1].reshape(rows_key, heads_here, head_size).astype(jnp.float32)  25.2 us
  transfers between devices with their start and end apart: 14, of which 14 were waited for; matrix products, arithmetic and copies ran while one was open for 3% of the time, Pallas kernels for 0%

commit v1 on v0

--- a/solution.py
+++ b/solution.py
@@ -2,6 +2,7 @@
 import jax.numpy as jnp
 from jax import lax
 from jax.sharding import PartitionSpec as P
+from jax.lax import all_gather
 
 HEAD_DIM = 64
 TOP = 2
@@ -141,7 +142,8 @@
             .astype(jnp.bfloat16)
         )
         attn_part = jnp.dot(context, w_out, preferred_element_type=jnp.float32)
-        mid = resid + lax.psum(attn_part, "rep")
+        start_strips_all_up = lambda xs: jnp.sum(all_gather(xs, "rep"), axis=0)
+        mid = resid + start_strips_all_up(attn_part)
         normed_mid = rms_scale(mid, gains[1]).astype(jnp.bfloat16)
         logits = jnp.dot(normed_mid, w_router, preferred_element_type=jnp.float32)
         expert_ids = jnp.arange(experts_all, dtype=jnp.int32)

time: 1010 us -> 967 us (0.957)
  waiting for transfers between devices: 619 us -> 579 us
    psum x3 -> x0, waiting for transfers between devices: 139 us -> none  [per_device(): mid = resid + lax.psum(attn_part, 'rep')]
    all_gather x0 -> x3, waiting for transfers between devices: none -> 93 us  [per_device(): start_strips_all_up = lambda xs: jnp.sum(all_gather(xs, 'rep'), axis=0)]
  transfers between devices with their start and end apart: 14 -> 14, of which waited for: 14 -> 14; matrix products, arithmetic and copies ran while one was open for 3% -> 2% of each run, Pallas kernels for 0% -> 0%
where the time goes in v1:
time: 967 us; the launch traced here: 964 us
  waiting for transfers between devices  579 us (60%)
  blocking collectives  147 us (15%)
  other arithmetic  78.9 us (8%)
  local copies, waits for them, and re-layouts  75.9 us (8%)
  matrix products  45.8 us (5%)
  starting transfers between devices  20.4 us (2%)
  between operations  16.4 us (2%)
    all_gather x3, waiting for transfers between devices, per_device(): piece = lax.all_gather(keys_vals, 'tok', axis=0, tiled=True)  249 us
    all_to_all x3, blocking collectives, per_device(): lax.all_to_all(copies, 'tok', split_axis=0, concat_axis=0, tiled=True)  147 us
    psum x3, waiting for transfers between devices, per_device(): expert_total = lax.psum(expert_local, 'rep')  126 us
    all_to_all x3, waiting for transfers between devices, per_device(): lax.all_to_all(jnp.einsum('secf,efd->secd', hidden, w_down, preferred_ele...  109 us
    all_gather x3, waiting for transfers between devices, per_device(): start_strips_all_up = lambda xs: jnp.sum(all_gather(xs, 'rep'), axis=0)  93 us
    slice x12, local copies, waits for them, and re-layouts, attend(): keys_vals[:, 1].reshape(rows_key, heads_here, head_size).astype(jnp.float32)  25.2 us
  transfers between devices with their start and end apart: 14, of which 14 were waited for; matrix products, arithmetic and copies ran while one was open for 2% of the time, Pallas kernels for 0%

profile of v1, /device:TPU:8, one launch (start us, length us, event | category | flops | bytes accessed | tf_op | source)
XLA Modules:
  0.0 964.3 jit_solution(7476454365511821823)
XLA Ops:
  17.8 82.5 %all-gather.10.cloned.1.call-done = bf16[4096,2,256]{0,2,1:T(8,128)(2,1)} async-done(((bf16[128,2,256]{0,2,1:T(8,128)(2,1)}), bf16[4096,2,256]{0,2,1:T(8,128)(2,1)}) %all-gather.10.cloned.1.call-update) | async-done | bytes 4194320 | tf_op jit(solution)/shard_map/all_gather | solution.py:121
  100.3 34.6 %while.54 = (s32[]{:T(128)}, f32[4,128]{1,0:T(4,128)S(1)}, f32[4,128]{1,0:T(4,128)S(1)}, f32[4,128,64]{1,2,0:T(8,128)}, s32[128]{0:T(128)}, /*index=5*/s32[4096]...) while((s32[]{:T(128)}, f32[4,128]{1,0:T(4,128)S(1)}, ...), condition=%wide.region_4.5_spmd.clone, body=%wide.region_1.4_spmd.clone.sunk | while | flops 476548736 | bytes 14800775 | solution.py:135
  140.4 31.3 %all-gather.16.cloned.1.call-done = f32[512,1024]{1,0:T(8,128)} async-done(((f32[128,1024]{1,0:T(8,128)}), f32[512,1024]{1,0:T(8,128)}) %all-gather.16.cloned.1.call-update) | async-done | bytes 2097168 | tf_op jit(solution)/shard_map/all_gather | solution.py:145
  174.4 49.1 %all_to_all.30 = bf16[32,1,20,1024]{3,2,1,0:T(8,128)(2,1)S(1)} all-to-all(bf16[32,1,20,1024]{3,2,1,0:T(8,128)(2,1)S(1)} %bitcast.396), channel_id=1, replica_groups=mesh['section'=2,'tok'=32,'rep'=4] {'tok'}, dimensions={0} | all-to-all | bytes 2621440 | tf_op jit(solution)/shard_map/all_to_all | solution.py:170
  228.2 5.6 all-to-all-start.1
  236.9 35.2 %all-to-all-done.1 = bf16[32,1,20,1024]{3,2,1,0:T(8,128)(2,1)S(1)} async-done(((bf16[32,1,20,1024]{3,2,1,0:T(8,128)(2,1)}), bf16[32,1,20,1024]{3,2,1,0:T(8,128)(2,1)S(1)}, u32[]{:S(2)}, u32[]{:S(2)}) %all-to-all-start.1) | async-done | bytes 1310752 | tf_op jit(solution)/shard_map/all_to_all | solution.py:175
  275.1 2.3 gather_fusion
  279.8 43.7 %all-reduce.4.cloned.1.call-done = f32[128,1024]{1,0:T(8,128)} async-done(((f32[128,1024]{1,0:T(8,128)}), f32[128,1024]{1,0:T(8,128)}) %all-reduce.4.cloned.1.call-update) | async-done | bytes 524304 | tf_op jit(solution)/shard_map/psum | solution.py:190
  331.2 83.1 %all-gather.12.cloned.1.call-done = bf16[4096,2,256]{0,2,1:T(8,128)(2,1)} async-done(((bf16[128,2,256]{0,2,1:T(8,128)(2,1)}), bf16[4096,2,256]{0,2,1:T(8,128)(2,1)}) %all-gather.12.cloned.1.call-update) | async-done | bytes 4194320 | tf_op jit(solution)/shard_map/all_gather | solution.py:121
  414.3 34.5 %while.55 = (s32[]{:T(128)}, f32[4,128]{1,0:T(4,128)S(1)}, f32[4,128]{1,0:T(4,128)S(1)}, f32[4,128,64]{1,2,0:T(8,128)}, s32[128]{0:T(128)}, /*index=5*/s32[4096]...) while((s32[]{:T(128)}, f32[4,128]{1,0:T(4,128)S(1)}, ...), condition=%wide.region_21.23_spmd.clone, body=%wide.region_18.22_spmd.clone.sunk | while | flops 476548736 | bytes 14800775 | solution.py:135
  456.8 28.7 %all-gather.18.cloned.1.call-done = f32[512,1024]{1,0:T(8,128)} async-done(((f32[128,1024]{1,0:T(8,128)}), f32[512,1024]{1,0:T(8,128)}) %all-gather.18.cloned.1.call-update) | async-done | bytes 2097168 | tf_op jit(solution)/shard_map/all_gather | solution.py:145
  489.0 49.1 %all_to_all.31 = bf16[32,1,20,1024]{3,2,1,0:T(8,128)(2,1)S(1)} all-to-all(bf16[32,1,20,1024]{3,2,1,0:T(8,128)(2,1)S(1)} %bitcast.397), channel_id=1, replica_groups=mesh['section'=2,'tok'=32,'rep'=4] {'tok'}, dimensions={0} | all-to-all | bytes 2621440 | tf_op jit(solution)/shard_map/all_to_all | solution.py:170
  542.8 5.7 all-to-all-start.3
  551.5 35.4 %all-to-all-done.3 = bf16[32,1,20,1024]{3,2,1,0:T(8,128)(2,1)S(1)} async-done(((bf16[32,1,20,1024]{3,2,1,0:T(8,128)(2,1)}), bf16[32,1,20,1024]{3,2,1,0:T(8,128)(2,1)S(1)}, u32[]{:S(2)}, u32[]{:S(2)}) %all-to-all-start.3) | async-done | bytes 1310752 | tf_op jit(solution)/shard_map/all_to_all | solution.py:175
  589.9 2.3 gather_fusion.1
  594.6 43.7 %all-reduce.6.cloned.1.call-done = f32[128,1024]{1,0:T(8,128)} async-done(((f32[128,1024]{1,0:T(8,128)}), f32[128,1024]{1,0:T(8,128)}) %all-reduce.6.cloned.1.call-update) | async-done | bytes 524304 | tf_op jit(solution)/shard_map/psum | solution.py:190
  646.2 82.9 %all-gather.14.cloned.1.call-done = bf16[4096,2,256]{0,2,1:T(8,128)(2,1)} async-done(((bf16[128,2,256]{0,2,1:T(8,128)(2,1)}), bf16[4096,2,256]{0,2,1:T(8,128)(2,1)}) %all-gather.14.cloned.1.call-update) | async-done | bytes 4194320 | tf_op jit(solution)/shard_map/all_gather | solution.py:121
  729.1 34.7 %while.56 = (s32[]{:T(128)}, f32[4,128]{1,0:T(4,128)S(1)}, f32[4,128]{1,0:T(4,128)S(1)}, f32[4,128,64]{1,2,0:T(8,128)}, s32[128]{0:T(128)}, /*index=5*/s32[4096]...) while((s32[]{:T(128)}, f32[4,128]{1,0:T(4,128)S(1)}, ...), condition=%wide.region_38.40_spmd.clone, body=%wide.region_35.39_spmd.clone.sunk | while | flops 476548736 | bytes 14800775 | solution.py:135
  767.5 32.9 %all-gather.20.cloned.1.call-done = f32[512,1024]{1,0:T(8,128)} async-done(((f32[128,1024]{1,0:T(8,128)}), f32[512,1024]{1,0:T(8,128)}) %all-gather.20.cloned.1.call-update) | async-done | bytes 2097168 | tf_op jit(solution)/shard_map/all_gather | solution.py:145
  805.2 49.1 %all_to_all.32 = bf16[32,1,20,1024]{3,2,1,0:T(8,128)(2,1)S(1)} all-to-all(bf16[32,1,20,1024]{3,2,1,0:T(8,128)(2,1)S(1)} %bitcast.398), channel_id=1, replica_groups=mesh['section'=2,'tok'=32,'rep'=4] {'tok'}, dimensions={0} | all-to-all | bytes 2621440 | tf_op jit(solution)/shard_map/all_to_all | solution.py:170
  858.9 5.8 all-to-all-start.5
  865.0 38.0 %all-to-all-done.5 = bf16[32,1,20,1024]{3,2,1,0:T(8,128)(2,1)} async-done(((bf16[32,1,20,1024]{3,2,1,0:T(8,128)(2,1)}), bf16[32,1,20,1024]{3,2,1,0:T(8,128)(2,1)}, u32[]{:S(2)}, u32[]{:S(2)}) %all-to-all-start.5) | async-done | bytes 1310752 | tf_op jit(solution)/shard_map/all_to_all | solution.py:175
  903.0 3.1 convert_reduce_fusion
  916.8 39.0 %all-reduce.8.cloned.1.call-done = f32[128,1024]{1,0:T(8,128)} async-done(((f32[128,1024]{1,0:T(8,128)}), f32[128,1024]{1,0:T(8,128)}) %all-reduce.8.cloned.1.call-update) | async-done | bytes 524304 | tf_op jit(solution)/shard_map/psum | solution.py:190
  (491 shorter events, 198.6 us)
Async XLA Ops:
  7.2 216.4 %copy-start = (bf16[1,1,1024,2,352]{2,4,3,1,0:T(8,128)(2,1)S(1)}, bf16[1,1,1024,2,352]{2,4,3,1,0:T(8,128)(2,1)}, u32[]{:S(2)}) copy-start(bf16[1,1,1024,2,352]{2,4,3,1,0:T(8,128)(2,1)} %param.26) | copy-start | bytes 4325380
  7.2 93.1 %all-gather.10.cloned.1.call-start = ((), (), s32[]{:S(2)}) async-start(), calls=%async_computation.6 | async-start | bytes 4325376 | tf_op jit(solution)/shard_map/all_gather | solution.py:121
  11.0 89.3 %copy-start.7 = (bf16[1,1024,3,256]{1,3,2,0:T(8,128)(2,1)}, bf16[1,1024,3,256]{1,3,2,0:T(8,128)(2,1)S(1)}, u32[]{:S(2)}) copy-start(bf16[1,1024,3,256]{1,3,2,0:T(8,128)(2,1)S(1)} %copy.83) | copy-start | bytes 4718596
  14.2 157.5 %all-gather.16.cloned.1.call-start = ((), (), s32[]{:S(2)}) async-start(), calls=%async_computation.12 | async-start | bytes 2621440 | tf_op jit(solution)/shard_map/all_gather | solution.py:145
  135.9 37.6 %copy-start.18 = (bf16[2,128,1024]{2,1,0:T(8,128)(2,1)S(1)}, bf16[2,128,1024]{2,1,0:T(8,128)(2,1)}, u32[]{:S(2)}) copy-start(bf16[2,128,1024]{2,1,0:T(8,128)(2,1)} %param.18) | copy-start | bytes 1572868
  228.2 43.9 %all-to-all-start.1 = ((bf16[32,1,20,1024]{3,2,1,0:T(8,128)(2,1)}), bf16[32,1,20,1024]{3,2,1,0:T(8,128)(2,1)S(1)}, u32[]{:S(2)}, u32[]{:S(2)}) async-start(bf16[32,1,20,1024]{3,2,1,0:T(8,128)(2,1)} %copy.87), calls=%async_computation.1 | async-start | bytes 3145728 | tf_op jit(solution)/shard_map/all_to_all | solution.py:175
  233.7 89.8 %all-reduce.4.cloned.1.call-start = ((), (), s32[]{:S(2)}) async-start(), calls=%async_computation.7 | async-start | bytes 1048576 | tf_op jit(solution)/shard_map/psum | solution.py:190
  278.8 50.2 %copy-start.8 = (bf16[1,1024,3,256]{1,3,2,0:T(8,128)(2,1)S(1)}, bf16[1,1024,3,256]{1,3,2,0:T(8,128)(2,1)}, u32[]{:S(2)}) copy-start(bf16[1,1024,3,256]{1,3,2,0:T(8,128)(2,1)} %copy-done.7) | copy-start | bytes 4718596
  278.8 50.2 %copy-start.36 = (f32[1,1,1024]{2,1,0:T(1,128)S(1)}, f32[1,1,1024]{2,1,0:T(1,128)}, u32[]{:S(2)}) copy-start(f32[1,1,1024]{2,1,0:T(1,128)} %copy-done.35) | copy-start | bytes 12292
  279.7 134.6 %all-gather.12.cloned.1.call-start = ((), (), s32[]{:S(2)}) async-start(), calls=%async_computation.8 | async-start | bytes 4325376 | tf_op jit(solution)/shard_map/all_gather | solution.py:121
  324.7 2.4 collective-permute-start
  330.5 155.0 %all-gather.18.cloned.1.call-start = ((), (), s32[]{:S(2)}) async-start(), calls=%async_computation.13 | async-start | bytes 2621440 | tf_op jit(solution)/shard_map/all_gather | solution.py:145
  542.8 44.0 %all-to-all-start.3 = ((bf16[32,1,20,1024]{3,2,1,0:T(8,128)(2,1)}), bf16[32,1,20,1024]{3,2,1,0:T(8,128)(2,1)S(1)}, u32[]{:S(2)}, u32[]{:S(2)}) async-start(bf16[32,1,20,1024]{3,2,1,0:T(8,128)(2,1)} %copy.93), calls=%async_computation.3 | async-start | bytes 3145728 | tf_op jit(solution)/shard_map/all_to_all | solution.py:175
  548.5 89.8 %all-reduce.6.cloned.1.call-start = ((), (), s32[]{:S(2)}) async-start(), calls=%async_computation.9 | async-start | bytes 1048576 | tf_op jit(solution)/shard_map/psum | solution.py:190
  594.5 49.2 %copy-start.9 = (bf16[1,1024,3,256]{1,3,2,0:T(8,128)(2,1)S(1)}, bf16[1,1024,3,256]{1,3,2,0:T(8,128)(2,1)}, u32[]{:S(2)}) copy-start(bf16[1,1024,3,256]{1,3,2,0:T(8,128)(2,1)} %copy-done.7) | copy-start | bytes 4718596
  594.5 49.2 %copy-start.37 = (f32[1,1,1024]{2,1,0:T(1,128)S(1)}, f32[1,1,1024]{2,1,0:T(1,128)}, u32[]{:S(2)}) copy-start(f32[1,1,1024]{2,1,0:T(1,128)} %copy-done.35) | copy-start | bytes 12292
  594.5 134.6 %all-gather.14.cloned.1.call-start = ((), (), s32[]{:S(2)}) async-start(), calls=%async_computation.10 | async-start | bytes 4325376 | tf_op jit(solution)/shard_map/all_gather | solution.py:121
  640.4 2.4 collective-permute-start.1
  645.3 155.2 %all-gather.20.cloned.1.call-start = ((), (), s32[]{:S(2)}) async-start(), calls=%async_computation.14 | async-start | bytes 2621440 | tf_op jit(solution)/shard_map/all_gather | solution.py:145
  764.6 37.6 %copy-start.14 = (bf16[128,1024]{1,0:T(8,128)(2,1)S(1)}, bf16[128,1024]{1,0:T(8,128)(2,1)}, u32[]{:S(2)}) copy-start(bf16[128,1024]{1,0:T(8,128)(2,1)} %copy-done.13) | copy-start | bytes 786436
  858.9 44.2 %all-to-all-start.5 = ((bf16[32,1,20,1024]{3,2,1,0:T(8,128)(2,1)}), bf16[32,1,20,1024]{3,2,1,0:T(8,128)(2,1)}, u32[]{:S(2)}, u32[]{:S(2)}) async-start(bf16[32,1,20,1024]{3,2,1,0:T(8,128)(2,1)} %copy.99), calls=%async_computation.5 | async-start | bytes 3145728 | tf_op jit(solution)/shard_map/all_to_all | solution.py:175
  864.6 91.1 %all-reduce.8.cloned.1.call-start = ((), (), s32[]{:S(2)}) async-start(), calls=%async_computation.11 | async-start | bytes 1048576 | tf_op jit(solution)/shard_map/psum | solution.py:190
  911.0 44.7 %copy-start.25 = (bf16[128,1024]{1,0:T(8,128)(2,1)S(1)}, bf16[128,1024]{1,0:T(8,128)(2,1)}, u32[]{:S(2)}) copy-start(bf16[128,1024]{1,0:T(8,128)(2,1)} %copy-done.24) | copy-start | bytes 786436
  912.0 45.0 %copy-start.26 = (bf16[1,128,1024]{2,1,0:T(8,128)(2,1)S(1)}, bf16[1,128,1024]{2,1,0:T(8,128)(2,1)}, u32[]{:S(2)}) copy-start(bf16[1,128,1024]{2,1,0:T(8,128)(2,1)} %get-tuple-element.669) | copy-start | bytes 786436
  (93 other events, 212.6 us)
Sparse Core Ops, SparseCore 0:
  14.3 85.9 all-gather.9
  138.2 33.4 all-gather.15
  279.8 43.6 all-reduce.3
  330.6 83.6 all-gather.11
  452.0 33.4 all-gather.17
  594.6 43.6 all-reduce.5
  645.4 83.6 all-gather.13
  766.9 33.4 all-gather.19
  912.1 43.6 all-reduce.7
